TPU v7x, 128 devices: a whole 4x4x4 slice. The times are simulated.
128 devices in a mesh: dp: 2 (over core), cent: 64 (over z, y, x).
Axes of the slice: x: 4, y: 4, z: 4, core: 2. Of those that a mesh axis runs over, the one named last changes fastest.
Arguments:
- points: bfloat16 [16384, 768], P(('dp', 'cent')), may hold values from -16 to 16
- centroids: float32 [32768, 768], P(('dp', 'cent')), may hold values from -1.5 to 1.5
Outputs:
- new_centroids: float32 [32768, 768], P(('dp', 'cent'))
- log_total: float32 [16384], P(('dp', 'cent'))
All inputs are finite; a program needn't handle non-finite values.
Results may differ from a plain program's by a relative error of at most 0.0088.
Values may be sent and summed in bfloat16 or wider, within the bound.
No kernel may reach another device: no remote copies, remote signals or barrier semaphores. Data moves between devices by JAX's collectives and lax.ppermute only.
A program may use at most 128 MiB of HBM per device.

v0:
```python
import math
import jax
import jax.numpy as jnp
from jax import lax
from jax.sharding import PartitionSpec as P

BLOCKS = 2


def score_block(members, cent_block, score_scale):
    sq_norm = jnp.sum(jnp.square(cent_block.astype(jnp.float32)), axis=1)
    products = lax.dot_general(
        members, cent_block, (((1,), (1,)), ((), ())), preferred_element_type=jnp.float32
    )
    return (2.0 * products - sq_norm[None, :]) * score_scale


def fold_stats(running, scores):
    old_max, old_sum = running
    new_max = jnp.maximum(old_max, jnp.max(scores, axis=1))
    new_sum = old_sum * jnp.exp(old_max - new_max) + jnp.sum(
        jnp.exp(scores - new_max[:, None]), axis=1
    )
    return (new_max, new_sum)


def on_device(points, centroids):
    feature_width = centroids.shape[1]
    own_rows = centroids.shape[0]
    dp_count = lax.axis_size("dp")
    score_scale = 7.0 / math.sqrt(feature_width)
    copies = centroids.astype(jnp.bfloat16)
    members = lax.all_gather(points, "cent", axis=0, tiled=True)
    member_rows = members.shape[0]
    start = (jnp.full((member_rows,), -1e30, jnp.float32), jnp.zeros((member_rows,), jnp.float32))
    part_rows = own_rows // BLOCKS
    gathered = lax.all_gather(copies, "dp", axis=0, tiled=True)
    running = start
    block_span = gathered.shape[0] // BLOCKS
    for index_j in range(BLOCKS):
        running = fold_stats(
            running,
            score_block(
                members, gathered[index_j * block_span : (index_j + 1) * block_span], score_scale
            ),
        )
    local_max, local_sum = running
    global_max = lax.pmax(local_max.astype(jnp.bfloat16), "cent").astype(local_max.dtype)
    global_sum = lax.psum(local_sum * jnp.exp(local_max - global_max), "cent")
    log_total = global_max + jnp.log(global_sum)
    arranged = gathered.reshape(dp_count, BLOCKS, part_rows, feature_width)
    sum_parts = []
    count_parts = []
    for index_j in range(BLOCKS):
        cent_block = arranged[:, index_j].reshape(dp_count * part_rows, feature_width)
        scores = score_block(members, cent_block, score_scale)
        weights = jnp.exp(scores - log_total[:, None]).astype(jnp.bfloat16)
        partial_sums = lax.dot_general(
            weights, members, (((0,), (0,)), ((), ())), preferred_element_type=jnp.float32
        )
        counts = jnp.sum(weights, axis=0, dtype=jnp.float32)
        owned_sums, owned_counts = (
            lax.psum_scatter(partial_sums, "dp", scatter_dimension=0, tiled=True),
            lax.psum_scatter(counts, "dp", scatter_dimension=0, tiled=True),
        )
        sum_parts.append(owned_sums)
        count_parts.append(owned_counts)
    own_sums = jnp.concatenate(sum_parts, axis=0)
    own_counts = jnp.concatenate(count_parts, axis=0)
    new_centroids = (own_sums + centroids) / (own_counts[:, None] + 1.0)
    own_points = points.shape[0]
    own_total = lax.dynamic_slice_in_dim(log_total, lax.axis_index("cent") * own_points, own_points)
    return (new_centroids, own_total)


def solution(mesh):
    placed = (P(("dp", "cent"), None), P(("dp", "cent"), None))
    return jax.shard_map(
        on_device,
        mesh=mesh,
        in_specs=placed,
        out_specs=(P(("dp", "cent"), None), P(("dp", "cent"))),
        check_vma=False,
    )
```

profile of v0, /device:TPU:1, one launch (start us, length us, event | category | flops | bytes accessed | tf_op | source)
XLA Modules:
  0.0 861.3 jit_solution(398983884775000078)
XLA Ops:
  7.2 0.0 all-gather.2.cloned.1.call-start
  7.2 0.7 all-gather.2.cloned.1.call-update
  7.9 0.0 reduce-scatter.5.cloned.1.call-start
  7.9 1.2 convert_element_type.35
  9.1 3.4 all_gather.7
  12.5 0.2 multiply_reduce_fusion.2
  12.7 0.2 multiply_reduce_fusion.3
  13.0 0.1 fusion.22
  13.0 91.7 %all-gather.2.cloned.1.call-done = bf16[8192,768]{1,0:T(8,128)(2,1)} async-done(((bf16[128,768]{1,0:T(8,128)(2,1)}), bf16[8192,768]{1,0:T(8,128)(2,1)}) %all-gather.2.cloned.1.call-update) | async-done | bytes 12582928 | tf_op jit(solution)/shard_map/all_gather | solution.py:33
  104.7 0.0 copy-start
  104.7 11.4 %fusion.23 = (f32[8192]{0:T(1024)S(1)}, f32[8192,256]{1,0:T(8,128)}) fusion(f32[256]{0:T(256)S(1)} %get-tuple-element.5, bf16[8192,768]{1,0:T(8,128)(2,1)} %all-gather.2.cloned.1.call-done, bf16[512,768]{1,0:T(8,128)(2,1)S(1)} %all_gather.7), kind=kOutput, calls=%fused_computation.39 | convolution fusion | flops 3229605888 | bytes 21398528 | tf_op jit(solution)/shard_map/dot_general | solution.py:12
  116.1 0.0 copy-done
  116.1 5.7 fusion.24
  121.9 291.5 %pmax.7 = bf16[8192]{0:T(1024)(128)(2,1)S(1)} all-reduce(bf16[8192]{0:T(1024)(128)(2,1)S(1)} %get-tuple-element.8), channel_id=1, replica_groups=mesh['dp'=2,'cent'=64] {'cent'}, use_global_device_ids=true, to_apply=%region_5.0 | all-reduce | flops 8192 | bytes 32768 | tf_op jit(solution)/shard_map/pmax | solution.py:48
  413.4 8.3 exponential_reduce_fusion
  421.7 286.7 %psum.7 = f32[8192]{0:T(1024)S(1)} all-reduce(f32[8192]{0:T(1024)S(1)} %fusion.18), channel_id=1, replica_groups=mesh['dp'=2,'cent'=64] {'cent'}, use_global_device_ids=true, to_apply=%region_8.0 | all-reduce | flops 8192 | bytes 65536 | tf_op jit(solution)/shard_map/psum | solution.py:49
  708.4 6.8 convert_reduce_fusion
  715.3 7.4 fusion.26
  722.6 0.0 reduce-scatter.5.cloned.1.call-update
  722.7 0.2 reduce-scatter.3.cloned.1.call-start
  722.9 6.8 convert_reduce_fusion.1
  729.7 0.0 copy-start.2
  729.7 0.0 copy-start.1
  729.7 7.5 fusion.25
  737.2 0.0 reduce-scatter.3.cloned.1.call-update
  737.3 0.0 copy-done.2
  737.3 0.6 dynamic-slice
  738.5 113.3 %all-reduce.2 = (f32[256]{0:T(256)S(1)}, f32[256]{0:T(256)S(1)}) all-reduce(f32[256]{0:T(256)S(1)} %get-tuple-element.17, f32[256]{0:T(256)S(1)} %get-tuple-element.19), channel_id=5, replica_groups=mesh['dp'=2,'cent'=64] {'dp'}, use_global_device_ids=true, to_apply=%region_15.0.clone | all-reduce | flops 512 | bytes 4096
  851.9 0.1 dynamic-slice.3
  851.9 0.1 dynamic-slice.1
  852.0 0.6 dynamic_slice.3
  852.6 0.0 reduce-scatter.5.cloned.1.call-done
  852.6 0.0 reduce-scatter.3.cloned.1.call-done
  852.6 0.0 copy-done.1
  852.7 2.1 fusion.14
  (4 shorter events, 0.1 us)
Async XLA Ops:
  7.2 97.6 %all-gather.2.cloned.1.call-start = ((), (), s32[]{:S(2)}) async-start(), calls=%async_computation.2 | async-start | bytes 12779520 | tf_op jit(solution)/shard_map/all_gather | solution.py:33
  7.9 844.7 %reduce-scatter.5.cloned.1.call-start = ((), (), s32[]{:S(2)}) async-start(), calls=%async_computation.4 | async-start | bytes 1179648 | tf_op jit(solution)/shard_map/reduce_scatter | solution.py:63
  104.7 11.4 %copy-start = (bf16[8192,768]{1,0:T(8,128)(2,1)S(1)}, bf16[8192,768]{1,0:T(8,128)(2,1)}, u32[]{:S(2)}) copy-start(bf16[8192,768]{1,0:T(8,128)(2,1)} %all-gather.2.cloned.1.call-done) | copy-start | bytes 37748740
  722.7 130.0 %reduce-scatter.3.cloned.1.call-start = ((), (), s32[]{:S(2)}) async-start(), calls=%async_computation.3 | async-start | bytes 1179648 | tf_op jit(solution)/shard_map/reduce_scatter | solution.py:63
  729.7 7.5 copy-start.2
  729.7 122.9 %copy-start.1 = (f32[256,768]{1,0:T(8,128)S(1)}, f32[256,768]{1,0:T(8,128)}, u32[]{:S(2)}) copy-start(f32[256,768]{1,0:T(8,128)} %param.3) | copy-start | bytes 2359300
Sparse Core Ops, SparseCore 0:
  10.7 93.9 all-gather.1
  722.8 114.9 reduce-scatter.4
  840.1 12.4 reduce-scatter.2
where the time goes:
time: 862 us; the launch traced here: 861 us
  blocking collectives  695 us (81%)
  waiting for transfers between devices  92.4 us (11%)
  matrix products  45.7 us (5%)
  between operations  14.5 us (2%)
  other arithmetic  12.1 us (1%)
    pmax x1, blocking collectives, on_device(): lax.pmax(local_max.astype(jnp.bfloat16), 'cent').astype(local_max.dtype)  292 us
    psum x1, blocking collectives, on_device(): global_sum = lax.psum(local_sum * jnp.exp(local_max - global_max), 'cent')  287 us
    unnamed x1, blocking collectives  113 us
    all_gather x1, waiting for transfers between devices, on_device(): members = lax.all_gather(points, 'cent', axis=0, tiled=True)  91.7 us
    dot_general x4, matrix products, score_block(): lax.dot_general(members, cent_block, (((1,), (1,)), ((), ())), preferred_...  30.8 us
  transfers between devices with their start and end apart: 3, of which 1 were waited for; matrix products, arithmetic and copies ran while one was open for 2% of the time, Pallas kernels for 0%

commit v1 on v0

--- a/solution.py
+++ b/solution.py
@@ -1,3 +1,4 @@
+import functools
 import math
 import jax
 import jax.numpy as jnp
@@ -5,6 +6,13 @@
 from jax.sharding import PartitionSpec as P
 
 BLOCKS = 2
+
+
+def _extend_cycles(q_in, chip_axis):
+    return lax.all_gather(q_in, chip_axis).sum(axis=0)
+
+
+run_vector = functools.partial(_extend_cycles, chip_axis="cent")
 
 
 def score_block(members, cent_block, score_scale):
@@ -46,7 +54,7 @@
         )
     local_max, local_sum = running
     global_max = lax.pmax(local_max.astype(jnp.bfloat16), "cent").astype(local_max.dtype)
-    global_sum = lax.psum(local_sum * jnp.exp(local_max - global_max), "cent")
+    global_sum = run_vector(local_sum * jnp.exp(local_max - global_max))
     log_total = global_max + jnp.log(global_sum)
     arranged = gathered.reshape(dp_count, BLOCKS, part_rows, feature_width)
     sum_parts = []

time: 862 us -> 586 us (0.68)
  blocking collectives: 695 us -> 299 us
  waiting for transfers between devices: 92.4 us -> 209 us
    psum x1 -> x0, blocking collectives: 287 us -> none  [on_device(): global_sum = lax.psum(local_sum * jnp.exp(local_max - global_max), 'cent')]
    all_gather x0 -> x1, waiting for transfers between devices: none -> 112 us  [_extend_cycles(): return lax.all_gather(q_in, chip_axis).sum(axis=0)]
    unnamed x1, blocking collectives: 113 us -> 4.24 us
  transfers between devices with their start and end apart: 3 -> 4, of which waited for: 1 -> 3; matrix products, arithmetic and copies ran while one was open for 2% -> 3% of each run, Pallas kernels for 0% -> 0%
where the time goes in v1:
time: 586 us; the launch traced here: 585 us
  blocking collectives  299 us (51%)
  waiting for transfers between devices  209 us (36%)
  matrix products  46 us (8%)
  between operations  14.5 us (2%)
  other arithmetic  12.8 us (2%)
    pmax x1, blocking collectives, on_device(): lax.pmax(local_max.astype(jnp.bfloat16), 'cent').astype(local_max.dtype)  292 us
    all_gather x1, waiting for transfers between devices, _extend_cycles(): return lax.all_gather(q_in, chip_axis).sum(axis=0)  112 us
    all_gather x1, waiting for transfers between devices, on_device(): members = lax.all_gather(points, 'cent', axis=0, tiled=True)  92 us
    dot_general x4, matrix products, score_block(): lax.dot_general(members, cent_block, (((1,), (1,)), ((), ())), preferred_...  30.8 us
    dot_general x2, matrix products, on_device(): lax.dot_general(weights, members, (((0,), (0,)), ((), ())), preferred_ele...  15.2 us
  transfers between devices with their start and end apart: 4, of which 3 were waited for; matrix products, arithmetic and copies ran while one was open for 3% of the time, Pallas kernels for 0%

profile of v1, /device:TPU:1, one launch (start us, length us, event | category | flops | bytes accessed | tf_op | source)
XLA Modules:
  0.0 585.4 jit_solution(12936786160581797606)
XLA Ops:
  7.2 0.0 all-gather.4.cloned.1.call-start
  7.2 0.7 all-gather.4.cloned.1.call-update
  7.9 0.0 all-gather.6.cloned.1.call-start
  7.9 1.2 convert_element_type.35
  9.1 3.4 all_gather.13
  12.5 0.2 multiply_reduce_fusion.2
  12.7 92.0 %all-gather.4.cloned.1.call-done = bf16[8192,768]{1,0:T(8,128)(2,1)} async-done(((bf16[128,768]{1,0:T(8,128)(2,1)}), bf16[8192,768]{1,0:T(8,128)(2,1)}) %all-gather.4.cloned.1.call-update) | async-done | bytes 12582928 | tf_op jit(solution)/shard_map/all_gather | solution.py:41
  104.7 0.0 copy-start
  104.7 11.4 %fusion.23 = (f32[8192]{0:T(1024)S(1)}, f32[8192,256]{1,0:T(8,128)}) fusion(f32[256]{0:T(256)S(1)} %get-tuple-element.5, bf16[8192,768]{1,0:T(8,128)(2,1)} %all-gather.4.cloned.1.call-done, bf16[512,768]{1,0:T(8,128)(2,1)S(1)} %all_gather.13), kind=kOutput, calls=%fused_computation.39 | convolution fusion | flops 3229605888 | bytes 21398528 | tf_op jit(solution)/shard_map/dot_general | solution.py:20
  116.1 0.0 copy-done
  116.1 5.7 fusion.24
  121.9 291.5 %pmax.7 = bf16[8192]{0:T(1024)(128)(2,1)S(1)} all-reduce(bf16[8192]{0:T(1024)(128)(2,1)S(1)} %get-tuple-element.8), channel_id=1, replica_groups=mesh['dp'=2,'cent'=64] {'cent'}, use_global_device_ids=true, to_apply=%region_5.0 | all-reduce | flops 8192 | bytes 32768 | tf_op jit(solution)/shard_map/pmax | solution.py:56
  413.4 8.3 %exponential_reduce_fusion = (f32[8192]{0:T(1024)S(1)}, f32[8192]{0:T(1024)S(1)}) fusion(f32[8192,256]{1,0:T(8,128)} %get-tuple-element.14, f32[8192]{0:T(1024)S(1)} %get-tuple-element.9, f32[8192,256]{1,0:T(8,128)} %get-tuple-element.16, f32[8192]{0:T(1024)S(1)} %get-tuple-element.12), kind=kLoop, calls=%fused_computation.20 | loop fusion | flops 8372224 | bytes 16908288 | tf_op jit(solution)/shard_map/reduce_sum | solution.py:29
  421.7 0.6 fusion.18
  422.3 0.0 all-gather.6.cloned.1.call-update
  422.3 0.0 reduce-scatter.5.cloned.1.call-start
  422.4 0.2 multiply_reduce_fusion.3
  422.6 0.8 fusion.22
  423.4 111.6 %all-gather.6.cloned.1.call-done = f32[524288]{0:T(1024)} async-done(((f32[8192]{0:T(1024)}), f32[524288]{0:T(1024)}) %all-gather.6.cloned.1.call-update) | async-done | bytes 2097168 | tf_op jit(solution)/shard_map/all_gather | solution.py:12
  535.0 1.7 reshape.45
  536.7 0.1 reduce_sum.86
  536.9 6.9 %convert_reduce_fusion = (f32[256]{0:T(256)S(1)}, bf16[8192,256]{1,0:T(8,128)(2,1)S(1)}) fusion(f32[8192]{0:T(1024)S(1)} %convert_add_fusion, f32[256]{0:T(256)S(1)} %bitcast.21, bf16[8192,768]{1,0:T(8,128)(2,1)} %all-gather.4.cloned.1.call-done, bf16[256,768]{1,0:T(8,128)(2,1)} %bitcast.19), kind=kOutput, calls=%fused_computation.18 | convolution fusion | flops 3235905280 | bytes 17205248 | tf_op jit(solution)/shard_map/dot_general | solution.py:20
  543.8 7.4 %fusion.26 = f32[256,768]{1,0:T(8,128)} fusion(bf16[8192,256]{1,0:T(8,128)(2,1)S(1)} %get-tuple-element.18, bf16[8192,768]{1,0:T(8,128)(2,1)} %all-gather.4.cloned.1.call-done), kind=kOutput, calls=%fused_computation.42 | convolution fusion | flops 3221225472 | bytes 17563648 | tf_op jit(solution)/shard_map/dot_general | solution.py:66
  551.1 0.0 reduce-scatter.5.cloned.1.call-update
  551.2 0.2 reduce-scatter.3.cloned.1.call-start
  551.4 6.8 %convert_reduce_fusion.1 = (f32[256]{0:T(256)S(1)}, bf16[8192,256]{1,0:T(8,128)(2,1)S(1)}) fusion(f32[8192]{0:T(1024)S(1)} %convert_add_fusion, f32[256]{0:T(256)S(1)} %bitcast.20, bf16[8192,768]{1,0:T(8,128)(2,1)} %all-gather.4.cloned.1.call-done, bf16[256,768]{1,0:T(8,128)(2,1)S(1)} %bitcast.18), kind=kOutput, calls=%fused_computation.19 | convolution fusion | flops 3235905280 | bytes 17205248 | tf_op jit(solution)/shard_map/dot_general | solution.py:20
  558.2 0.0 copy-start.2
  558.2 0.0 copy-start.1
  558.2 7.9 %fusion.25 = f32[256,768]{1,0:T(8,128)} fusion(bf16[8192,256]{1,0:T(8,128)(2,1)S(1)} %get-tuple-element.20, bf16[8192,768]{1,0:T(8,128)(2,1)} %all-gather.4.cloned.1.call-done), kind=kOutput, calls=%fused_computation.41 | convolution fusion | flops 3221225472 | bytes 17563648 | tf_op jit(solution)/shard_map/dot_general | solution.py:66
  566.1 0.0 reduce-scatter.3.cloned.1.call-update
  566.1 0.0 copy-done.2
  566.1 0.6 dynamic-slice
  567.4 4.2 all-reduce.2
  571.6 0.1 dynamic-slice.3
  571.7 0.1 dynamic-slice.1
  571.8 0.6 dynamic_slice.3
  572.4 0.0 reduce-scatter.5.cloned.1.call-done
  572.4 4.3 reduce-scatter.3.cloned.1.call-done
  576.7 0.0 copy-done.1
  576.7 2.1 fusion.14
  (3 shorter events, 0.0 us)
Async XLA Ops:
  7.2 97.6 %all-gather.4.cloned.1.call-start = ((), (), s32[]{:S(2)}) async-start(), calls=%async_computation.2 | async-start | bytes 12779520 | tf_op jit(solution)/shard_map/all_gather | solution.py:41
  7.9 527.1 %all-gather.6.cloned.1.call-start = ((), (), s32[]{:S(2)}) async-start(), calls=%async_computation.5 | async-start | bytes 2129920 | tf_op jit(solution)/shard_map/all_gather | solution.py:12
  104.7 11.4 %copy-start = (bf16[8192,768]{1,0:T(8,128)(2,1)S(1)}, bf16[8192,768]{1,0:T(8,128)(2,1)}, u32[]{:S(2)}) copy-start(bf16[8192,768]{1,0:T(8,128)(2,1)} %all-gather.4.cloned.1.call-done) | copy-start | bytes 37748740
  422.3 150.1 %reduce-scatter.5.cloned.1.call-start = ((), (), s32[]{:S(2)}) async-start(), calls=%async_computation.4 | async-start | bytes 1179648 | tf_op jit(solution)/shard_map/reduce_scatter | solution.py:71
  551.2 25.6 %reduce-scatter.3.cloned.1.call-start = ((), (), s32[]{:S(2)}) async-start(), calls=%async_computation.3 | async-start | bytes 1179648 | tf_op jit(solution)/shard_map/reduce_scatter | solution.py:71
  558.2 7.9 %copy-start.2 = (u32[128]{0:T(128)S(1)}, u32[128]{0:T(128)}, u32[]{:S(2)}) copy-start(u32[128]{0:T(128)} %constant.25) | copy-start | bytes 1540
  558.2 18.5 %copy-start.1 = (f32[256,768]{1,0:T(8,128)S(1)}, f32[256,768]{1,0:T(8,128)}, u32[]{:S(2)}) copy-start(f32[256,768]{1,0:T(8,128)} %param.3) | copy-start | bytes 2359300
Sparse Core Ops, SparseCore 0:
  10.7 93.9 all-gather.3
  422.4 112.4 all-gather.5
  551.3 10.5 reduce-scatter.4
  566.2 10.4 reduce-scatter.2
